TPU v7x, 512 devices: a whole 4x4x16 slice. The times are simulated.
512 devices in a mesh: win: 16 (over z_hi, y, core), tm: 32 (over z_lo, x).
Axes of the slice: x: 4, y: 4, z: 16 (z_hi: 2, z_lo: 8; z = z_hi * 8 + z_lo), core: 2. Of those that a mesh axis runs over, the one named last changes fastest.
Arguments:
- frame_inputs: bfloat16 [16, 4096, 2048], P('win', 'tm'), may hold values from -6 to 6
- gate_channels: bfloat16 [16, 4096, 2048], P('win', 'tm'), may hold values from -6 to 6
- state_input_weight: bfloat16 [16, 4096, 128], P('win', 'tm'), may hold values from -6 to 6
- state_output_weight: bfloat16 [16, 4096, 128], P('win', 'tm'), may hold values from -0.59765625 to 0.59765625
- head_decay_codes: int32 [2, 32], replicated, may hold values from 0 to 7
- loss_frames: int32 [16, 4096], P('win', 'tm'), may hold values 0 or 1
- gated_norm_gain: float32 [2048], replicated, may hold values from 0.1 to 1.9
- output_weight: bfloat16 [2048, 1024], P(None, 'tm'), may hold values from -0.125 to 0.125
- seam_taper_shape: int32 [16], replicated, may hold values from 0 to 3
Outputs:
- mixed: bfloat16 [16, 4096, 1024], P('win', 'tm')
All inputs are finite; a program needn't handle non-finite values. No bound on the sum of `loss_frames` on one device may be relied on, other than what follows from the above.
Results may differ from a plain program's by a relative error of at most 0.0059.
Values may be sent and summed in bfloat16 or wider, within the bound.
No kernel may reach another device: no remote copies, remote signals or barrier semaphores. Data moves between devices by JAX's collectives and lax.ppermute only.
A program may use at most 192 MiB of HBM per device.

v0:
```python
import jax
import jax.numpy as jnp
from jax import lax
from jax.sharding import PartitionSpec as P

H = 32
P_SIZE = 64
N = 128
SEAM_DEVS = 4
STATE_LOSS = 0.4
EPSILON = 1e-05


def prefix(value, axis, join, neutral, backward):
    count, mine = (lax.axis_size(axis), lax.axis_index(axis))
    pieces = jax.tree.map(lambda part: lax.all_gather(part, axis), value)
    if backward:
        pieces = jax.tree.map(lambda part: part[::-1], pieces)
        mine = count - 1 - mine
    total = jax.tree.map(
        lambda part, zero: jnp.full_like(part, 0) + jnp.asarray(zero, part.dtype), value, neutral
    )

    def lap(position, total):
        longer = join(total, jax.tree.map(lambda part: part[position], pieces))
        return jax.tree.map(lambda new, old: jnp.where(position < mine, new, old), longer, total)

    return lax.fori_loop(0, count - 1, lap, total)


def shifted(array, axis, by):
    count = lax.axis_size(axis)
    pairs = [(i, i + by) for i in range(count) if 0 <= i + by < count]
    return lax.ppermute(array, axis, pairs)


def decay_rates(head_decay_codes, window_length):
    codes_float = head_decay_codes.astype(jnp.float32)
    quick = jnp.exp2(-codes_float) / 32.0
    gentle = jnp.exp2(5.0 - codes_float) / window_length
    return jnp.where(head_decay_codes < 4, quick, gentle)


def taper_weight(taper_code, position, seam_length):
    spread = (position.astype(jnp.float32) + 0.5) / seam_length
    shapes = jnp.stack(
        [
            spread,
            spread * spread * (3.0 - 2.0 * spread),
            jnp.sin(0.5 * jnp.pi * spread) ** 2,
            spread**3 * (spread * (6.0 * spread - 15.0) + 10.0),
        ]
    )
    kind_index = jnp.arange(4).reshape((4,) + (1,) * spread.ndim)
    selected = kind_index == jnp.expand_dims(taper_code, 0)
    return jnp.sum(jnp.where(selected, shapes, 0.0), axis=0)


def link_states(earlier, later):
    return (earlier[0] * later[0], later[0][:, None, None] * earlier[1] + later[1])


def per_device(
    frame_inputs,
    gate_channels,
    state_input_weight,
    state_output_weight,
    head_decay_codes,
    loss_frames,
    gated_norm_gain,
    output_weight,
    seam_taper_shape,
):
    frames = frame_inputs[0]
    frame_count = frames.shape[0]
    chain_length = lax.axis_size("tm")
    window_length = frame_count * chain_length
    seam_length = SEAM_DEVS * frame_count
    stride_length = window_length - seam_length
    reach = chain_length - SEAM_DEVS
    group_count = H // 4
    decay_rate_pair = decay_rates(head_decay_codes, window_length)
    loss_float = loss_frames[0].astype(jnp.float32)[:, None]
    forward_log_decay = -(decay_rate_pair[0][None, :] + STATE_LOSS * loss_float)
    backward_log_decay = -(decay_rate_pair[1][None, :] + STATE_LOSS * loss_float)
    running_fwd = jnp.cumsum(forward_log_decay, axis=0)
    running_bwd = jnp.flip(jnp.cumsum(jnp.flip(backward_log_decay, 0), axis=0), 0)
    b_rows = state_input_weight[0]
    c_rows = state_output_weight[0]
    head_frames = frames.reshape(frame_count, H, P_SIZE)
    b_float = b_rows.astype(jnp.float32)[:, None, :]
    weighted_fwd = (jnp.exp(running_fwd[-1][None, :] - running_fwd)[:, :, None] * b_float).astype(
        jnp.bfloat16
    )
    weighted_bwd = (jnp.exp(running_bwd[0][None, :] - running_bwd)[:, :, None] * b_float).astype(
        jnp.bfloat16
    )
    fresh_fwd = jnp.einsum(
        "shp,shn->hpn", head_frames, weighted_fwd, preferred_element_type=jnp.float32
    )
    fresh_bwd = jnp.einsum(
        "shp,shn->hpn", head_frames, weighted_bwd, preferred_element_type=jnp.float32
    )
    identity_pair = (jnp.ones((H,), jnp.float32), jnp.zeros((H, P_SIZE, N), jnp.float32))
    _, state_fwd = prefix(
        (jnp.exp(running_fwd[-1]), fresh_fwd), "tm", link_states, identity_pair, False
    )
    _, state_bwd = prefix(
        (jnp.exp(running_bwd[0]), fresh_bwd), "tm", link_states, identity_pair, True
    )
    scores = jnp.dot(c_rows, b_rows.T, preferred_element_type=jnp.float32)
    lower_mask = jnp.arange(frame_count)[:, None] >= jnp.arange(frame_count)[None, :]

    def group_mix(group_items):
        group_fwd, group_bwd, group_frames = group_items
        exponent = jnp.where(
            lower_mask[None],
            group_fwd[:, :, None] - group_fwd[:, None, :],
            group_bwd[:, :, None] - group_bwd[:, None, :],
        )
        mixing = (scores[None] * jnp.exp(exponent)).astype(jnp.bfloat16)
        return jnp.einsum("hts,shp->thp", mixing, group_frames, preferred_element_type=jnp.float32)

    grouped_fwd = running_fwd.T.reshape(group_count, 4, frame_count)
    grouped_bwd = running_bwd.T.reshape(group_count, 4, frame_count)
    grouped_frames = head_frames.reshape(frame_count, group_count, 4, P_SIZE).transpose(1, 0, 2, 3)
    local_groups = lax.map(group_mix, (grouped_fwd, grouped_bwd, grouped_frames))
    local_part = local_groups.transpose(1, 0, 2, 3).reshape(frame_count, H, P_SIZE)
    c_float = c_rows.astype(jnp.float32)
    carried_fwd = jnp.exp(running_fwd)[:, :, None] * jnp.einsum(
        "hpn,tn->thp", state_fwd, c_float, precision=lax.Precision.HIGHEST
    )
    carried_bwd = jnp.exp(running_bwd)[:, :, None] * jnp.einsum(
        "hpn,tn->thp", state_bwd, c_float, precision=lax.Precision.HIGHEST
    )
    summed = local_part + carried_fwd + carried_bwd
    gated_rows = summed * jax.nn.silu(gate_channels[0].astype(jnp.float32)).reshape(
        frame_count, H, P_SIZE
    )
    inverse_rms = lax.rsqrt(jnp.mean(gated_rows * gated_rows, axis=-1, keepdims=True) + EPSILON)
    normed = (
        (gated_rows * inverse_rms).reshape(frame_count, H * P_SIZE) * gated_norm_gain[None, :]
    ).astype(jnp.bfloat16)
    projected_rows = jnp.dot(
        normed,
        lax.all_gather(output_weight, "tm", axis=1, tiled=True),
        preferred_element_type=jnp.float32,
    ).astype(jnp.bfloat16)
    across_previous = shifted(projected_rows, "win", 1)
    from_previous = shifted(across_previous, "tm", -reach)
    across_next = shifted(projected_rows, "win", -1)
    from_next = shifted(across_next, "tm", reach)
    window_index = lax.axis_index("win")
    window_total = lax.axis_size("win")
    position = lax.axis_index("tm") * frame_count + jnp.arange(frame_count)
    next_window = jnp.minimum(window_index + 1, window_total - 1)
    head_fade = taper_weight(seam_taper_shape[window_index], position, seam_length)[:, None]
    tail_fade = taper_weight(seam_taper_shape[next_window], position - stride_length, seam_length)[
        :, None
    ]
    own_rows = projected_rows.astype(jnp.float32)
    head_mix = head_fade * own_rows + (1.0 - head_fade) * from_previous.astype(jnp.float32)
    tail_mix = tail_fade * from_next.astype(jnp.float32) + (1.0 - tail_fade) * own_rows
    use_head = (position < seam_length) & (window_index > 0)
    use_tail = (position >= stride_length) & (window_index < window_total - 1)
    mixed = jnp.where(use_head[:, None], head_mix, jnp.where(use_tail[:, None], tail_mix, own_rows))
    return mixed.astype(jnp.bfloat16)[None]


def solution(mesh):
    in_specs = (
        P("win", "tm", None),
        P("win", "tm", None),
        P("win", "tm", None),
        P("win", "tm", None),
        P(),
        P("win", "tm"),
        P(),
        P(None, "tm"),
        P(),
    )
    out_specs = P("win", "tm", None)
    return jax.shard_map(
        per_device, mesh=mesh, in_specs=in_specs, out_specs=out_specs, check_vma=False
    )
```

profile of v0, /device:TPU:480, one launch (start us, length us, event | category | flops | bytes accessed | tf_op | source)
XLA Modules:
  0.0 1035.5 jit_solution(9995021697445433449)
XLA Ops:
  10.5 1.8 convolution_bitcast_fusion.4
  13.0 1.8 convolution_bitcast_fusion.3
  15.7 98.1 %all-gather.2 = f32[32,1,32]{2,1,0:T(1,128)S(1)} all-gather(f32[1,1,32]{2,1,0:T(1,128)S(1)} %get-tuple-element.328), channel_id=1, replica_groups=mesh['win'=16,'tm'=32] {'tm'}, dimensions={0}, use_global_device_ids=true | all-gather | bytes 4224 | tf_op jit(solution)/shard_map/all_gather | solution.py:16
  114.1 8.2 while.39
  122.3 116.8 %all-gather.3 = f32[32,1,32]{2,1,0:T(1,128)S(1)} all-gather(f32[1,1,32]{2,1,0:T(1,128)S(1)} %get-tuple-element.324), channel_id=1, replica_groups=mesh['win'=16,'tm'=32] {'tm'}, dimensions={0}, use_global_device_ids=true | all-gather | bytes 4224 | tf_op jit(solution)/shard_map/all_gather | solution.py:16
  242.3 139.6 %all-gather.10.cloned.1.call-done = f32[1024,64,128]{2,1,0:T(8,128)} async-done(((f32[32,64,128]{2,1,0:T(8,128)}), f32[1024,64,128]{2,1,0:T(8,128)}) %all-gather.10.cloned.1.call-update) | async-done | bytes 33554448 | tf_op jit(solution)/shard_map/all_gather | solution.py:16
  381.9 46.8 %while.40 = (s32[]{:T(128)}, f32[32,64,128]{2,1,0:T(8,128)S(1)}, s32[]{:T(128)}, f32[32,32]{1,0:T(8,128)S(1)}, f32[32,32,64,128]{3,2,1,0:T(8,128)}, /*index=5*/s32[]{:T(128)}, s32[]{:T(128)}) while((s32[]{:T(128)}, f32[32,64,128]{2,1,0:T(8,128)S(1)}, s32[]{:T(128)}, f32[32,32]{1,0:T(8,128)S(1)}, f32[32,32,64,128]{3,2,1,0:T(8,128)}, ...), condition=%wide.region_6.7_spmd.clone, body=%wide.region_5.6_spmd.clone.sunk | while | flops 1048580 | bytes 3146217 | solution.py:28
  383.4 1.5 fusion.53
  384.9 1.5 fusion.53
  386.4 1.5 fusion.53
  387.9 1.5 fusion.53
  389.4 1.5 fusion.53
  390.9 1.5 fusion.53
  392.5 1.5 fusion.53
  394.0 1.5 fusion.53
  395.5 1.5 fusion.53
  398.5 1.5 fusion.53
  400.0 1.5 fusion.53
  401.5 1.5 fusion.53
  403.0 1.5 fusion.53
  404.5 1.5 fusion.53
  406.0 1.5 fusion.53
  407.5 1.5 fusion.53
  409.1 1.5 fusion.53
  410.6 1.5 fusion.53
  412.1 1.5 fusion.53
  413.6 1.5 fusion.53
  415.1 1.5 fusion.53
  416.6 1.5 fusion.53
  418.1 1.5 fusion.53
  419.6 1.5 fusion.53
  421.2 1.5 fusion.53
  422.7 1.5 fusion.53
  424.2 1.5 fusion.53
  425.7 1.5 fusion.53
  427.2 1.5 fusion.53
  428.7 324.4 %all-gather.12.cloned.1.call-done = f32[1024,64,128]{2,1,0:T(8,128)} async-done(((f32[32,64,128]{2,1,0:T(8,128)}), f32[1024,64,128]{2,1,0:T(8,128)}) %all-gather.12.cloned.1.call-update) | async-done | bytes 33554448 | tf_op jit(solution)/shard_map/all_gather | solution.py:16
  753.1 23.3 %rev.16 = f32[32,32,64,128]{3,2,1,0:T(8,128)} reverse(f32[32,32,64,128]{3,2,1,0:T(8,128)} %bitcast.116), dimensions={0} | reverse | bytes 67108864 | tf_op jit(solution)/shard_map/rev | solution.py:18
  776.4 1.8 fusion.17
  778.2 46.8 %while.41 = (s32[]{:T(128)}, f32[32,64,128]{2,1,0:T(8,128)S(1)}, s32[]{:T(128)}, f32[32,32]{1,0:T(8,128)S(1)}, f32[32,32,64,128]{3,2,1,0:T(8,128)}, /*index=5*/s32[]{:T(128)}, s32[]{:T(128)}) while((s32[]{:T(128)}, f32[32,64,128]{2,1,0:T(8,128)S(1)}, s32[]{:T(128)}, f32[32,32]{1,0:T(8,128)S(1)}, f32[32,32,64,128]{3,2,1,0:T(8,128)}, ...), condition=%wide.region_8.9_spmd.clone, body=%wide.region_7.8_spmd.clone.sunk | while | flops 1048580 | bytes 3146217 | solution.py:28
  778.3 1.6 fusion.54
  779.9 1.5 fusion.54
  781.4 1.5 fusion.54
  782.9 1.5 fusion.54
  784.4 1.5 fusion.54
  785.9 1.5 fusion.54
  787.4 1.5 fusion.54
  788.9 1.5 fusion.54
  790.4 1.5 fusion.54
  791.9 1.5 fusion.54
  794.9 1.5 fusion.54
  797.9 1.5 fusion.54
  805.5 1.5 fusion.54
  810.0 1.5 fusion.54
  813.0 1.5 fusion.54
  820.5 1.5 fusion.54
  826.4 145.4 %all-gather.8.cloned.1.call-done = bf16[2048,1024]{0,1:T(8,128)(2,1)} async-done(((bf16[2048,32]{0,1:T(8,128)(2,1)}), bf16[2048,1024]{0,1:T(8,128)(2,1)}) %all-gather.8.cloned.1.call-update) | async-done | bytes 4194320 | tf_op jit(solution)/shard_map/all_gather | solution.py:146
  971.8 3.7 convolution_convert_fusion
  975.5 1.9 collective-permute-start
  977.4 14.5 %collective-permute-start.2 = (bf16[128,1024]{1,0:T(8,128)(2,1)S(1)}, bf16[128,1024]{1,0:T(8,128)(2,1)S(1)}, u32[]{:S(2)}, u32[]{:S(2)}) collective-permute-start(bf16[128,1024]{1,0:T(8,128)(2,1)S(1)} %convolution_convert_fusion), channel_id=1, source_target_pairs={{32,0},{64,32},{96,64},{128,96},{160,128},{192,160},{224,192},{256... | collective-permute-start | bytes 786440 | tf_op jit(solution)/shard_map/ppermute | solution.py:34
  992.0 2.0 collective-permute-done
  994.0 19.1 %collective-permute-start.1 = (bf16[128,1024]{1,0:T(8,128)(2,1)S(1)}, bf16[128,1024]{1,0:T(8,128)(2,1)S(1)}, u32[]{:S(2)}, u32[]{:S(2)}) collective-permute-start(bf16[128,1024]{1,0:T(8,128)(2,1)S(1)} %collective-permute-done), channel_id=1, source_target_pairs={{28,0},{29,1},{30,2},{31,3},{60,32},{61,33},{62,34},{63,35},{92,64... | collective-permute-start | bytes 786440 | tf_op jit(solution)/shard_map/ppermute | solution.py:34
  1014.4 2.5 collective-permute-done.1
  1016.9 11.0 %collective-permute-done.3 = bf16[128,1024]{1,0:T(8,128)(2,1)S(1)} collective-permute-done((bf16[128,1024]{1,0:T(8,128)(2,1)S(1)}, bf16[128,1024]{1,0:T(8,128)(2,1)S(1)}, u32[]{:S(2)}, u32[]{:S(2)}) %collective-permute-start.3) | collective-permute-done | bytes 262176 | tf_op jit(solution)/shard_map/ppermute | solution.py:34
  (166 shorter events, 46.2 us)
Async XLA Ops:
  6.5 107.4 %copy-start = (bf16[1,128,128]{2,1,0:T(8,128)(2,1)S(1)}, bf16[1,128,128]{2,1,0:T(8,128)(2,1)}, u32[]{:S(2)}) copy-start(bf16[1,128,128]{2,1,0:T(8,128)(2,1)} %param.18) | copy-start | bytes 98308
  6.5 107.4 %copy-start.3 = (bf16[1,128,128]{2,1,0:T(8,128)(2,1)S(1)}, bf16[1,128,128]{2,1,0:T(8,128)(2,1)}, u32[]{:S(2)}) copy-start(bf16[1,128,128]{2,1,0:T(8,128)(2,1)} %param.17) | copy-start | bytes 98308
  6.5 375.4 %all-gather.10.cloned.1.call-start = ((), (), s32[]{:S(2)}) async-start(), calls=%async_computation.1 | async-start | bytes 34603008 | tf_op jit(solution)/shard_map/all_gather | solution.py:16
  12.3 226.8 %copy-start.2 = (bf16[1,128,2048]{2,1,0:T(8,128)(2,1)S(1)}, bf16[1,128,2048]{2,1,0:T(8,128)(2,1)}, u32[]{:S(2)}) copy-start(bf16[1,128,2048]{2,1,0:T(8,128)(2,1)} %param.16) | copy-start | bytes 1572868
  12.4 227.9 %copy-start.5 = (s32[16]{0:T(128)S(1)}, s32[16]{0:T(128)}, u32[]{:S(2)}) copy-start(s32[16]{0:T(128)} %param.23) | copy-start | bytes 196
  12.4 740.7 %all-gather.12.cloned.1.call-start = ((), (), s32[]{:S(2)}) async-start(), calls=%async_computation.2 | async-start | bytes 34603008 | tf_op jit(solution)/shard_map/all_gather | solution.py:16
  14.8 956.9 %all-gather.8.cloned.1.call-start = ((), (), s32[]{:S(2)}) async-start(), calls=%async_computation | async-start | bytes 4325376 | tf_op jit(solution)/shard_map/all_gather | solution.py:146
  778.2 46.8 %copy-start.1 = (f32[1,128,2048]{1,2,0:T(8,128)S(1)}, f32[1,128,2048]{1,2,0:T(8,128)}, u32[]{:S(2)}) copy-start(f32[1,128,2048]{1,2,0:T(8,128)} %copy.55) | copy-start | bytes 3145732
  825.0 1.0 copy-start.4
  975.5 18.5 %collective-permute-start = (bf16[128,1024]{1,0:T(8,128)(2,1)S(1)}, bf16[128,1024]{1,0:T(8,128)(2,1)S(1)}, u32[]{:S(2)}, u32[]{:S(2)}) collective-permute-start(bf16[128,1024]{1,0:T(8,128)(2,1)S(1)} %convolution_convert_fusion), channel_id=1, source_target_pairs={{0,32},{32,64},{64,96},{96,128},{128,160},{160,192},{192,224},{224... | collective-permute-start | bytes 786440 | tf_op jit(solution)/shard_map/ppermute | solution.py:34
  977.4 35.7 %collective-permute-start.2 = (bf16[128,1024]{1,0:T(8,128)(2,1)S(1)}, bf16[128,1024]{1,0:T(8,128)(2,1)S(1)}, u32[]{:S(2)}, u32[]{:S(2)}) collective-permute-start(bf16[128,1024]{1,0:T(8,128)(2,1)S(1)} %convolution_convert_fusion), channel_id=1, source_target_pairs={{32,0},{64,32},{96,64},{128,96},{160,128},{192,160},{224,192},{256... | collective-permute-start | bytes 786440 | tf_op jit(solution)/shard_map/ppermute | solution.py:34
  994.0 22.9 %collective-permute-start.1 = (bf16[128,1024]{1,0:T(8,128)(2,1)S(1)}, bf16[128,1024]{1,0:T(8,128)(2,1)S(1)}, u32[]{:S(2)}, u32[]{:S(2)}) collective-permute-start(bf16[128,1024]{1,0:T(8,128)(2,1)S(1)} %collective-permute-done), channel_id=1, source_target_pairs={{28,0},{29,1},{30,2},{31,3},{60,32},{61,33},{62,34},{63,35},{92,64... | collective-permute-start | bytes 786440 | tf_op jit(solution)/shard_map/ppermute | solution.py:34
  1013.1 14.9 %collective-permute-start.3 = (bf16[128,1024]{1,0:T(8,128)(2,1)S(1)}, bf16[128,1024]{1,0:T(8,128)(2,1)S(1)}, u32[]{:S(2)}, u32[]{:S(2)}) collective-permute-start(bf16[128,1024]{1,0:T(8,128)(2,1)S(1)} %collective-permute-done.2), channel_id=1, source_target_pairs={{0,28},{1,29},{2,30},{3,31},{32,60},{33,61},{34,62},{35,63},{64,92... | collective-permute-start | bytes 786440 | tf_op jit(solution)/shard_map/ppermute | solution.py:34
Sparse Core Ops, SparseCore 0:
  12.5 369.4 all-gather.9
  384.0 369.0 all-gather.11
  755.2 216.5 all-gather.7
where the time goes:
time: 1040 us
  waiting for transfers between devices  626 us (60%)
  blocking collectives  215 us (21%)
  other arithmetic  96.9 us (9%)
  starting transfers between devices  36.8 us (4%)
  local copies, waits for them, and re-layouts  27.7 us (3%)
  matrix products  18.1 us (2%)
  between operations  13.4 us (1%)
    all_gather x2, waiting for transfers between devices, prefix(): pieces = jax.tree.map(lambda part: lax.all_gather(part, axis), value)  464 us
    all_gather x2, blocking collectives, prefix(): pieces = jax.tree.map(lambda part: lax.all_gather(part, axis), value)  215 us
    all_gather x1, waiting for transfers between devices, per_device(): lax.all_gather(output_weight, 'tm', axis=1, tiled=True)  145 us
    select_n x62, other arithmetic, lap(): jnp.where(position < mine, new, old)  91 us
    ppermute x4, starting transfers between devices, shifted(): return lax.ppermute(array, axis, pairs)  36.7 us
    rev x2, local copies, waits for them, and re-layouts, prefix(): pieces = jax.tree.map(lambda part: part[::-1], pieces)  23.3 us
  transfers between devices with their start and end apart: 7, of which 6 were waited for; matrix products, arithmetic and copies ran while one was open for 13% of the time, Pallas kernels for 0%

commit v1 on v0

--- a/solution.py
+++ b/solution.py
@@ -143,7 +143,9 @@
     ).astype(jnp.bfloat16)
     projected_rows = jnp.dot(
         normed,
-        lax.all_gather(output_weight, "tm", axis=1, tiled=True),
+        jnp.concatenate(
+            lax.all_to_all(jnp.stack([output_weight] * lax.axis_size("tm")), "tm", 0, 0), axis=1
+        ),
         preferred_element_type=jnp.float32,
     ).astype(jnp.bfloat16)
     across_previous = shifted(projected_rows, "win", 1)

time: 1040 us -> 1070 us (1.029)
  blocking collectives: 215 us -> 381 us
  waiting for transfers between devices: 626 us -> 481 us
    all_gather x2, blocking collectives: 215 us -> 381 us  [prefix(): pieces = jax.tree.map(lambda part: lax.all_gather(part, axis), value)]
    all_gather x1 -> x0, waiting for transfers between devices: 145 us -> none  [per_device(): lax.all_gather(output_weight, 'tm', axis=1, tiled=True)]
    all_to_all x0 -> x1, starting transfers between devices: none -> 12.8 us  [per_device(): lax.all_to_all(jnp.stack([output_weight] * lax.axis_size('tm')), 'tm', 0, 0)]
  transfers between devices with their start and end apart: 7 -> 7, of which waited for: 6 -> 5; matrix products, arithmetic and copies ran while one was open for 13% -> 13% of each run, Pallas kernels for 0% -> 0%
where the time goes in v1:
time: 1070 us; the launch traced here: 1060 us
  waiting for transfers between devices  481 us (45%)
  blocking collectives  381 us (36%)
  other arithmetic  96.6 us (9%)
  starting transfers between devices  39.6 us (4%)
  local copies, waits for them, and re-layouts  30.3 us (3%)
  matrix products  19.1 us (2%)
  between operations  13.6 us (1%)
    all_gather x2, waiting for transfers between devices, prefix(): pieces = jax.tree.map(lambda part: lax.all_gather(part, axis), value)  465 us
    all_gather x2, blocking collectives, prefix(): pieces = jax.tree.map(lambda part: lax.all_gather(part, axis), value)  381 us
    select_n x62, other arithmetic, lap(): jnp.where(position < mine, new, old)  90.8 us
    ppermute x4, starting transfers between devices, shifted(): return lax.ppermute(array, axis, pairs)  26.7 us
    rev x2, local copies, waits for them, and re-layouts, prefix(): pieces = jax.tree.map(lambda part: part[::-1], pieces)  23.3 us
  transfers between devices with their start and end apart: 7, of which 5 were waited for; matrix products, arithmetic and copies ran while one was open for 13% of the time, Pallas kernels for 0%

profile of v1, /device:TPU:480, one launch (start us, length us, event | category | flops | bytes accessed | tf_op | source)
XLA Modules:
  0.0 1063.5 jit_solution(11479082685687124059)
XLA Ops:
  10.5 1.8 convolution_bitcast_fusion.4
  13.0 1.8 convolution_bitcast_fusion.3
  14.8 2.5 stack.7
  17.4 12.8 %all-to-all-start = ((bf16[32,2048,32]{1,2,0:T(8,128)(2,1)}), bf16[32,2048,32]{1,2,0:T(8,128)(2,1)}, u32[]{:S(2)}, u32[]{:S(2)}) async-start(bf16[32,2048,32]{1,2,0:T(8,128)(2,1)} %stack.7), calls=%async_computation | async-start | bytes 8388608 | tf_op jit(solution)/shard_map/all_to_all | solution.py:147
  30.3 274.9 %all-gather.3 = f32[32,1,32]{2,1,0:T(1,128)S(1)} all-gather(f32[1,1,32]{2,1,0:T(1,128)S(1)} %get-tuple-element.324), channel_id=1, replica_groups=mesh['win'=16,'tm'=32] {'tm'}, dimensions={0}, use_global_device_ids=true | all-gather | bytes 4224 | tf_op jit(solution)/shard_map/all_gather | solution.py:16
  307.2 106.4 %all-gather.2 = f32[32,1,32]{2,1,0:T(1,128)S(1)} all-gather(f32[1,1,32]{2,1,0:T(1,128)S(1)} %get-tuple-element.328), channel_id=1, replica_groups=mesh['win'=16,'tm'=32] {'tm'}, dimensions={0}, use_global_device_ids=true | all-gather | bytes 4224 | tf_op jit(solution)/shard_map/all_gather | solution.py:16
  415.3 8.2 while.39
  423.5 84.9 %all-gather.7.cloned.1.call-done = f32[1024,64,128]{2,1,0:T(8,128)} async-done(((f32[32,64,128]{2,1,0:T(8,128)}), f32[1024,64,128]{2,1,0:T(8,128)}) %all-gather.7.cloned.1.call-update) | async-done | bytes 33554448 | tf_op jit(solution)/shard_map/all_gather | solution.py:16
  508.4 46.5 %while.40 = (s32[]{:T(128)}, f32[32,64,128]{2,1,0:T(8,128)S(1)}, s32[]{:T(128)}, f32[32,32]{1,0:T(8,128)S(1)}, f32[32,32,64,128]{3,2,1,0:T(8,128)}, /*index=5*/s32[]{:T(128)}, s32[]{:T(128)}) while((s32[]{:T(128)}, f32[32,64,128]{2,1,0:T(8,128)S(1)}, s32[]{:T(128)}, f32[32,32]{1,0:T(8,128)S(1)}, f32[32,32,64,128]{3,2,1,0:T(8,128)}, ...), condition=%wide.region_6.7_spmd.clone, body=%wide.region_5.6_spmd.clone.sunk | while | flops 1048580 | bytes 3146217 | solution.py:28
  509.9 1.5 fusion.52
  511.4 1.5 fusion.52
  512.9 1.5 fusion.52
  514.4 1.5 fusion.52
  515.9 1.5 fusion.52
  517.4 1.5 fusion.52
  518.9 1.5 fusion.52
  520.4 1.5 fusion.52
  521.9 1.5 fusion.52
  523.4 1.5 fusion.52
  524.9 1.5 fusion.52
  526.4 1.5 fusion.52
  527.9 1.5 fusion.52
  529.4 1.5 fusion.52
  532.5 1.5 fusion.52
  534.0 1.5 fusion.52
  535.5 1.5 fusion.52
  537.0 1.5 fusion.52
  538.5 1.5 fusion.52
  540.0 1.5 fusion.52
  541.5 1.5 fusion.52
  543.0 1.5 fusion.52
  544.5 1.5 fusion.52
  546.0 1.5 fusion.52
  547.5 1.5 fusion.52
  549.0 1.5 fusion.52
  550.5 1.5 fusion.52
  552.0 1.5 fusion.52
  553.5 1.5 fusion.52
  555.0 380.1 %all-gather.9.cloned.1.call-done = f32[1024,64,128]{2,1,0:T(8,128)} async-done(((f32[32,64,128]{2,1,0:T(8,128)}), f32[1024,64,128]{2,1,0:T(8,128)}) %all-gather.9.cloned.1.call-update) | async-done | bytes 33554448 | tf_op jit(solution)/shard_map/all_gather | solution.py:16
  935.0 23.3 %rev.16 = f32[32,32,64,128]{3,2,1,0:T(8,128)} reverse(f32[32,32,64,128]{3,2,1,0:T(8,128)} %bitcast.116), dimensions={0} | reverse | bytes 67108864 | tf_op jit(solution)/shard_map/rev | solution.py:18
  958.3 2.8 fusion.17
  961.2 46.7 %while.41 = (s32[]{:T(128)}, f32[32,64,128]{2,1,0:T(8,128)S(1)}, s32[]{:T(128)}, f32[32,32]{1,0:T(8,128)S(1)}, f32[32,32,64,128]{3,2,1,0:T(8,128)}, /*index=5*/s32[]{:T(128)}, s32[]{:T(128)}) while((s32[]{:T(128)}, f32[32,64,128]{2,1,0:T(8,128)S(1)}, s32[]{:T(128)}, f32[32,32]{1,0:T(8,128)S(1)}, f32[32,32,64,128]{3,2,1,0:T(8,128)}, ...), condition=%wide.region_8.9_spmd.clone, body=%wide.region_7.8_spmd.clone.sunk | while | flops 1048580 | bytes 3146217 | solution.py:28
  961.2 1.6 fusion.53
  962.8 1.5 fusion.53
  964.3 1.5 fusion.53
  965.8 1.5 fusion.53
  967.3 1.5 fusion.53
  968.8 1.5 fusion.53
  970.4 1.5 fusion.53
  971.9 1.5 fusion.53
  974.9 1.5 fusion.53
  976.4 1.5 fusion.53
  977.9 1.5 fusion.53
  979.4 1.5 fusion.53
  980.9 1.5 fusion.53
  982.4 1.5 fusion.53
  983.9 1.5 fusion.53
  1009.1 3.7 convolution_convert_fusion
  1012.8 1.9 collective-permute-start
  1014.8 14.5 %collective-permute-start.2 = (bf16[128,1024]{1,0:T(8,128)(2,1)S(1)}, bf16[128,1024]{1,0:T(8,128)(2,1)S(1)}, u32[]{:S(2)}, u32[]{:S(2)}) collective-permute-start(bf16[128,1024]{1,0:T(8,128)(2,1)S(1)} %convolution_convert_fusion), channel_id=1, source_target_pairs={{32,0},{64,32},{96,64},{128,96},{160,128},{192,160},{224,192},{256... | collective-permute-start | bytes 786440 | tf_op jit(solution)/shard_map/ppermute | solution.py:34
  1029.3 2.3 collective-permute-done
  1031.7 9.1 collective-permute-start.1
  1042.1 2.5 collective-permute-done.1
  1044.6 11.0 %collective-permute-done.3 = bf16[128,1024]{1,0:T(8,128)(2,1)S(1)} collective-permute-done((bf16[128,1024]{1,0:T(8,128)(2,1)S(1)}, bf16[128,1024]{1,0:T(8,128)(2,1)S(1)}, u32[]{:S(2)}, u32[]{:S(2)}) %collective-permute-start.3) | collective-permute-done | bytes 262176 | tf_op jit(solution)/shard_map/ppermute | solution.py:34
  (170 shorter events, 47.0 us)
Async XLA Ops:
  6.5 408.6 %copy-start = (bf16[1,128,128]{2,1,0:T(8,128)(2,1)S(1)}, bf16[1,128,128]{2,1,0:T(8,128)(2,1)}, u32[]{:S(2)}) copy-start(bf16[1,128,128]{2,1,0:T(8,128)(2,1)} %param.18) | copy-start | bytes 98308
  6.5 8.3 copy-start.4
  6.5 501.9 %all-gather.7.cloned.1.call-start = ((), (), s32[]{:S(2)}) async-start(), calls=%async_computation.1 | async-start | bytes 34603008 | tf_op jit(solution)/shard_map/all_gather | solution.py:16
  12.4 922.7 %all-gather.9.cloned.1.call-start = ((), (), s32[]{:S(2)}) async-start(), calls=%async_computation.2 | async-start | bytes 34603008 | tf_op jit(solution)/shard_map/all_gather | solution.py:16
  17.3 287.9 %copy-start.3 = (bf16[1,128,2048]{2,1,0:T(8,128)(2,1)S(1)}, bf16[1,128,2048]{2,1,0:T(8,128)(2,1)}, u32[]{:S(2)}) copy-start(bf16[1,128,2048]{2,1,0:T(8,128)(2,1)} %param.16) | copy-start | bytes 1572868
  17.3 289.1 %copy-start.6 = (f32[2048]{0:T(1024)S(1)}, f32[2048]{0:T(1024)}, u32[]{:S(2)}) copy-start(f32[2048]{0:T(1024)} %param.21) | copy-start | bytes 24580
  17.3 289.2 %copy-start.7 = (s32[16]{0:T(128)S(1)}, s32[16]{0:T(128)}, u32[]{:S(2)}) copy-start(s32[16]{0:T(128)} %param.23) | copy-start | bytes 196
  17.3 397.8 %copy-start.5 = (bf16[1,128,128]{2,1,0:T(8,128)(2,1)S(1)}, bf16[1,128,128]{2,1,0:T(8,128)(2,1)}, u32[]{:S(2)}) copy-start(bf16[1,128,128]{2,1,0:T(8,128)(2,1)} %param.17) | copy-start | bytes 98308
  17.4 991.8 %all-to-all-start = ((bf16[32,2048,32]{1,2,0:T(8,128)(2,1)}), bf16[32,2048,32]{1,2,0:T(8,128)(2,1)}, u32[]{:S(2)}, u32[]{:S(2)}) async-start(bf16[32,2048,32]{1,2,0:T(8,128)(2,1)} %stack.7), calls=%async_computation | async-start | bytes 8388608 | tf_op jit(solution)/shard_map/all_to_all | solution.py:147
  961.2 46.7 %copy-start.1 = (f32[128,32,64]{0,2,1:T(8,128)S(1)}, f32[128,32,64]{0,2,1:T(8,128)}, u32[]{:S(2)}) copy-start(f32[128,32,64]{0,2,1:T(8,128)} %fusion.17) | copy-start | bytes 3145732
  961.2 46.7 %copy-start.2 = (f32[1,128,2048]{1,2,0:T(8,128)S(1)}, f32[1,128,2048]{1,2,0:T(8,128)}, u32[]{:S(2)}) copy-start(f32[1,128,2048]{1,2,0:T(8,128)} %copy.56) | copy-start | bytes 3145732
  1012.8 18.8 %collective-permute-start = (bf16[128,1024]{1,0:T(8,128)(2,1)S(1)}, bf16[128,1024]{1,0:T(8,128)(2,1)S(1)}, u32[]{:S(2)}, u32[]{:S(2)}) collective-permute-start(bf16[128,1024]{1,0:T(8,128)(2,1)S(1)} %convolution_convert_fusion), channel_id=1, source_target_pairs={{0,32},{32,64},{64,96},{96,128},{128,160},{160,192},{192,224},{224... | collective-permute-start | bytes 786440 | tf_op jit(solution)/shard_map/ppermute | solution.py:34
  1014.8 26.0 %collective-permute-start.2 = (bf16[128,1024]{1,0:T(8,128)(2,1)S(1)}, bf16[128,1024]{1,0:T(8,128)(2,1)S(1)}, u32[]{:S(2)}, u32[]{:S(2)}) collective-permute-start(bf16[128,1024]{1,0:T(8,128)(2,1)S(1)} %convolution_convert_fusion), channel_id=1, source_target_pairs={{32,0},{64,32},{96,64},{128,96},{160,128},{192,160},{224,192},{256... | collective-permute-start | bytes 786440 | tf_op jit(solution)/shard_map/ppermute | solution.py:34
  1031.7 12.9 %collective-permute-start.1 = (bf16[128,1024]{1,0:T(8,128)(2,1)S(1)}, bf16[128,1024]{1,0:T(8,128)(2,1)S(1)}, u32[]{:S(2)}, u32[]{:S(2)}) collective-permute-start(bf16[128,1024]{1,0:T(8,128)(2,1)S(1)} %collective-permute-done), channel_id=1, source_target_pairs={{28,0},{29,1},{30,2},{31,3},{60,32},{61,33},{62,34},{63,35},{92,64... | collective-permute-start | bytes 786440 | tf_op jit(solution)/shard_map/ppermute | solution.py:34
  1040.8 14.9 %collective-permute-start.3 = (bf16[128,1024]{1,0:T(8,128)(2,1)S(1)}, bf16[128,1024]{1,0:T(8,128)(2,1)S(1)}, u32[]{:S(2)}, u32[]{:S(2)}) collective-permute-start(bf16[128,1024]{1,0:T(8,128)(2,1)S(1)} %collective-permute-done.2), channel_id=1, source_target_pairs={{0,28},{1,29},{2,30},{3,31},{32,60},{33,61},{34,62},{35,63},{64,92... | collective-permute-start | bytes 786440 | tf_op jit(solution)/shard_map/ppermute | solution.py:34
Sparse Core Ops, SparseCore 0:
  12.5 495.8 all-gather.6
  510.5 424.5 all-gather.8
